TPU v7x, 256 devices: a whole 4x4x8 slice. The times are simulated.
256 devices in a mesh: dp: 8 (over y, z_lo), seq: 32 (over z_hi, x, core).
Axes of the slice: x: 4, y: 4, z: 8 (z_hi: 4, z_lo: 2; z = z_hi * 2 + z_lo), core: 2. Of those that a mesh axis runs over, the one named last changes fastest.
Arguments:
- tokens: bfloat16 [8, 256, 128, 512], P('dp', None, 'seq'), may hold values from -6 to 6
- patch_mask: int32 [8, 256, 128], P('dp', None, 'seq'), may hold values 0 or 1
- mask_token: float32 [512], replicated, may hold values from -6 to 6
- gain: float32 [512], replicated, may hold values from 0.1 to 1.9
- w_qkv: bfloat16 [512, 1536], replicated, may hold values from -0.25 to 0.25
- w_out: bfloat16 [512, 512], replicated, may hold values from -0.25 to 0.25
- block_ids: int32 [256], replicated, may hold values from 0 to 3, as said below
- temporal_mask: int32 [8, 8], replicated, may hold values from 0 to 1, as said below
- cotangent: bfloat16 [8, 256, 128, 512], P('dp', None, 'seq'), may hold values from -6 to 6
Outputs:
- layer_out: bfloat16 [8, 256, 128, 512], P('dp', None, 'seq')
- qkv_grad: float32 [1536, 512], P('seq')
- out_grad: float32 [512, 512], P('seq')
Inputs may be any that keep to these rules, and one draw needn't show every extreme that they name: `block_ids`: each block id is held by exactly 64 electrodes. `temporal_mask`: every diagonal entry is 1.
All inputs are finite; a program needn't handle non-finite values. No bound on the sum of `patch_mask` on one device may be relied on, other than what follows from the above.
Results may differ from a plain program's by a relative error of at most 0.0092.
Values may be sent and summed in bfloat16 or wider, within the bound.
No kernel may reach another device: no remote copies, remote signals or barrier semaphores. Data moves between devices by JAX's collectives and lax.ppermute only.
A program may use at most 128 MiB of HBM per device.

v0:
```python
import math

import jax
import jax.numpy as jnp
from jax import lax
from jax.sharding import PartitionSpec as P

P_SIZE = 128
HEADS = 8
HEAD_DIM = 64
EB = 64
TB = 16


NORM_EPS = 1e-05


def normed_input(tokens, patch_mask, mask_token, gain):
    masked = jnp.where(patch_mask[..., None] == 1, mask_token, tokens.astype(jnp.float32))
    row_mean = jnp.mean(masked, axis=-1, keepdims=True)
    centred = masked - row_mean
    spread = jnp.mean(centred * centred, axis=-1, keepdims=True)
    normed = (centred * lax.rsqrt(spread + NORM_EPS) * gain).astype(jnp.bfloat16)
    return (masked, normed)


def forward_attend(queries, key_rows, values, allowed, factor):
    scores = (
        jnp.einsum("anhd,amhd->ahnm", queries, key_rows, preferred_element_type=jnp.float32)
        * factor
    )
    exponent = jnp.exp(scores) * allowed
    weights = exponent / jnp.sum(exponent, axis=-1, keepdims=True)
    rounded = weights.astype(jnp.bfloat16)
    output = jnp.einsum(
        "ahnm,amhd->anhd", rounded, values, preferred_element_type=jnp.float32
    ).astype(jnp.bfloat16)
    return (output, weights, rounded)


def backward_attend(queries, key_rows, values, weights, rounded, grad_out, factor):
    grad_values = jnp.einsum(
        "ahnm,anhd->amhd", rounded, grad_out, preferred_element_type=jnp.float32
    ).astype(jnp.bfloat16)
    grad_weights = jnp.einsum(
        "anhd,amhd->ahnm", grad_out, values, preferred_element_type=jnp.float32
    )
    inner_sum = jnp.sum(grad_weights * weights, axis=-1, keepdims=True)
    grad_scores = (weights * (grad_weights - inner_sum)).astype(jnp.bfloat16)
    grad_queries = (
        jnp.einsum("ahnm,amhd->anhd", grad_scores, key_rows, preferred_element_type=jnp.float32)
        * factor
    ).astype(jnp.bfloat16)
    grad_keys = (
        jnp.einsum("ahnm,anhd->amhd", grad_scores, queries, preferred_element_type=jnp.float32)
        * factor
    ).astype(jnp.bfloat16)
    return (grad_queries, grad_keys, grad_values)


def to_blocks(tensor, block_order, block_size):
    record_count, electrodes, local_patches = tensor.shape[:3]
    trailing = tensor.shape[3:]
    picked = jnp.take(tensor, block_order, axis=1)
    picked = picked.reshape(
        (record_count, electrodes // block_size, block_size, local_patches) + trailing
    )
    picked = jnp.moveaxis(picked, 3, 2)
    return picked.reshape(
        (record_count * (electrodes // block_size) * local_patches, block_size) + trailing
    )


def from_blocks(tensor, inverse, record_count, electrodes, local_patches):
    block_size = tensor.shape[1]
    trailing = tensor.shape[2:]
    restored = tensor.reshape(
        (record_count, electrodes // block_size, local_patches, block_size) + trailing
    )
    restored = jnp.moveaxis(restored, 2, 3).reshape(
        (record_count, electrodes, local_patches) + trailing
    )
    return jnp.take(restored, inverse, axis=1)


def shards(tokens, patch_mask, mask_token, gain, w_qkv, w_out, block_ids, temporal_mask, cotangent):
    record_count, electrodes, local_patches, model_width = tokens.shape
    half_width = model_width // 2
    heads_half = HEADS // 2
    factor = HEAD_DIM ** (-0.5)
    onehot = (jnp.arange(P_SIZE)[:, None] // TB == jnp.arange(P_SIZE // TB)[None, :]).astype(
        jnp.float32
    )
    time_allowed = jnp.dot(jnp.dot(onehot, temporal_mask.astype(jnp.float32)), onehot.T)
    same_block = (block_ids[:, None] == block_ids[None, :]).astype(jnp.float32)
    masked, normed = normed_input(tokens, patch_mask, mask_token, gain)
    normed_flat = normed.reshape(-1, model_width)
    group_columns = 3 * half_width
    time_part = jnp.dot(
        normed_flat, w_qkv[:, group_columns:], preferred_element_type=jnp.float32
    ).astype(jnp.bfloat16)
    time_part = time_part.reshape(record_count, electrodes, local_patches, group_columns)
    regrouped = lax.all_to_all(time_part, SEQ, split_axis=1, concat_axis=2, tiled=True)
    projected = jnp.dot(
        normed_flat, w_qkv[:, :group_columns], preferred_element_type=jnp.float32
    ).astype(jnp.bfloat16)
    projected = projected.reshape(electrodes, local_patches, 3, heads_half, HEAD_DIM)
    spatial = jnp.transpose(projected, (1, 0, 2, 3, 4))
    space_out, space_weights, space_rounded = forward_attend(
        spatial[:, :, 0], spatial[:, :, 1], spatial[:, :, 2], same_block, factor
    )
    items = regrouped.shape[0]
    owned = regrouped.shape[1]
    split_heads = regrouped.reshape(items * owned, P_SIZE, 3, heads_half, HEAD_DIM)
    time_out, time_weights, time_rounded = forward_attend(
        split_heads[:, :, 0], split_heads[:, :, 1], split_heads[:, :, 2], time_allowed, factor
    )
    time_out = time_out.reshape(items, owned, P_SIZE, half_width)
    time_back = lax.all_to_all(time_out, SEQ, split_axis=2, concat_axis=1, tiled=True)
    space_back = jnp.transpose(space_out, (1, 0, 2, 3)).reshape(
        record_count, electrodes, local_patches, half_width
    )
    attended = jnp.concatenate([space_back, time_back], axis=-1)
    attended_flat = attended.reshape(-1, model_width)
    layer_out = (
        masked.reshape(-1, model_width)
        + jnp.dot(attended_flat, w_out, preferred_element_type=jnp.float32)
    ).astype(jnp.bfloat16)
    layer_out = layer_out.reshape(tokens.shape)
    cot_flat = cotangent.reshape(-1, model_width)
    out_grad = jnp.einsum("tc,td->cd", cot_flat, attended_flat, preferred_element_type=jnp.float32)
    attended_grad = jnp.einsum(
        "td,cd->tc", cot_flat, w_out, preferred_element_type=jnp.float32
    ).astype(jnp.bfloat16)
    attended_grad = attended_grad.reshape(record_count, electrodes, local_patches, model_width)
    space_grad = jnp.transpose(
        attended_grad[0, :, :, :half_width].reshape(electrodes, local_patches, heads_half, HEAD_DIM),
        (1, 0, 2, 3),
    )
    space_grads = backward_attend(
        spatial[:, :, 0],
        spatial[:, :, 1],
        spatial[:, :, 2],
        space_weights,
        space_rounded,
        space_grad,
        factor,
    )
    spatial_grad = jnp.transpose(jnp.stack(space_grads, axis=2), (1, 0, 2, 3, 4))
    spatial_grad = spatial_grad.reshape(-1, 3 * half_width)
    time_grad = lax.all_to_all(
        attended_grad[..., half_width:], SEQ, split_axis=1, concat_axis=2, tiled=True
    )
    owned = time_grad.shape[1]
    split_heads = regrouped.reshape(record_count * owned, P_SIZE, 3, heads_half, HEAD_DIM)
    unused_out, time_weights, time_rounded = forward_attend(
        split_heads[:, :, 0], split_heads[:, :, 1], split_heads[:, :, 2], time_allowed, factor
    )
    time_grads = backward_attend(
        split_heads[:, :, 0],
        split_heads[:, :, 1],
        split_heads[:, :, 2],
        time_weights,
        time_rounded,
        time_grad.reshape(record_count * owned, P_SIZE, heads_half, HEAD_DIM),
        factor,
    )
    temporal_grad = jnp.stack(time_grads, axis=2).reshape(
        record_count, owned, P_SIZE, 3 * half_width
    )
    temporal_back = lax.all_to_all(
        temporal_grad, SEQ, split_axis=2, concat_axis=1, tiled=True
    ).reshape(-1, 3 * half_width)
    space_qkv_grad = jnp.einsum(
        "tc,td->cd", spatial_grad, normed_flat, preferred_element_type=jnp.float32
    )
    time_qkv_grad = jnp.einsum(
        "tc,td->cd", temporal_back, normed_flat, preferred_element_type=jnp.float32
    )
    qkv_grad = jnp.concatenate([space_qkv_grad, time_qkv_grad], axis=0)
    groups = lax.axis_size(SEQ)
    grad_scale = 1.0 / math.sqrt(
        record_count * lax.axis_size("dp") * electrodes * local_patches * groups
    )
    rows_qkv = qkv_grad.shape[0] // groups
    rows_out = model_width // groups
    stacked = jnp.concatenate(
        [
            qkv_grad.reshape(groups, rows_qkv, model_width),
            out_grad.reshape(groups, rows_out, model_width),
        ],
        axis=1,
    )
    share = reduce_share(stacked, groups, lax.axis_size("dp"))
    return (layer_out, share[:rows_qkv] * grad_scale, share[rows_qkv:] * grad_scale)


def reduce_share(stacked, groups, members):
    cores = lax.axis_size("core")
    chips = groups // cores
    rows, width = stacked.shape[1:]
    core = lax.axis_index("core")
    blocks = stacked.reshape(chips, cores, rows, width)
    keep = lax.dynamic_index_in_dim(blocks, core, 1, keepdims=False)
    send = lax.dynamic_index_in_dim(blocks, 1 - core, 1, keepdims=False)
    swapped = lax.ppermute(send.astype(jnp.bfloat16), "core", [(0, 1), (1, 0)])
    summed = (keep + swapped.astype(jnp.float32)).astype(jnp.bfloat16)
    gathered = lax.all_to_all(summed, ("zh", "x"), split_axis=0, concat_axis=0, tiled=True)
    summed = jnp.sum(gathered.astype(jnp.float32), axis=0)
    bit = 1
    while bit < members:
        pairs = [(i, i ^ bit) for i in range(members)]
        summed = summed + lax.ppermute(summed, "dp", pairs)
        bit *= 2
    return summed


SEQ = ("zh", "x", "core")


def solution(mesh):
    dp_size, seq_size = mesh.devices.shape
    split = jax.sharding.Mesh(
        mesh.devices.reshape(dp_size, seq_size // 8, 4, 2), ("dp",) + SEQ
    )
    return jax.shard_map(
        shards,
        mesh=split,
        in_specs=(
            P("dp", None, SEQ, None),
            P("dp", None, SEQ),
            P(),
            P(),
            P(),
            P(),
            P(),
            P(),
            P("dp", None, SEQ, None),
        ),
        out_specs=(P("dp", None, SEQ, None), P(SEQ, None), P(SEQ, None)),
        check_vma=False,
    )
```

profile of v0, /device:TPU:2, one launch (start us, length us, event | category | flops | bytes accessed | tf_op | source)
XLA Modules:
  0.0 245.2 jit_solution(11920462638657109205)
XLA Ops:
  6.4 11.7 %all-to-all-start.2 = ((bf16[1,256,4,256]{3,2,0,1:T(4,128)(2,1)}), bf16[1,256,4,256]{3,2,0,1:T(4,128)(2,1)S(1)}, u32[]{:S(2)}, u32[]{:S(2)}) async-start(bf16[1,256,4,256]{3,2,0,1:T(4,128)(2,1)} %slice.63), calls=%async_computation.2 | async-start | bytes 1048576 | tf_op jit(solution)/shard_map/all_to_all | solution.py:151
  21.1 2.7 %multiply_convert_fusion.2 = (bf16[1,256,4,512]{3,2,1,0:T(4,128)(2,1)S(1)}, f32[1,256,4,512]{3,2,1,0:T(4,128)}) fusion(f32[512]{0:T(512)S(1)} %copy-done.24, f32[256,4]{1,0:T(8,128)S(1)} %add_rsqrt_fusion, f32[256,4]{1,0:T(8,128)S(1)} %broadcast_multiply_fusion, bf16[1,256,4,512]{3,2,1,0:T(4,128)(2,1)S(1)} %copy-done.4, f32[512]{0:T(512)S(1)} %copy-done.21, ...), kind=kLoop, calls=%fused_computation.21 | loop fusion | flops 3145728 | bytes 4207616 | tf_op jit(solution)/shard_map/convert_element_type | solution.py:23
  24.9 2.4 convolution_convert_fusion
  28.8 6.2 %all-to-all-done.2 = bf16[1,256,4,256]{3,2,0,1:T(4,128)(2,1)S(1)} async-done(((bf16[1,256,4,256]{3,2,0,1:T(4,128)(2,1)}), bf16[1,256,4,256]{3,2,0,1:T(4,128)(2,1)S(1)}, u32[]{:S(2)}, u32[]{:S(2)}) %all-to-all-start.2) | async-done | bytes 524320 | tf_op jit(solution)/shard_map/all_to_all | solution.py:151
  35.0 5.6 %all-to-all-start = ((bf16[1,256,4,768]{3,2,0,1:T(4,128)(2,1)}), bf16[1,256,4,768]{3,2,0,1:T(4,128)(2,1)}, u32[]{:S(2)}, u32[]{:S(2)}) async-start(bf16[1,256,4,768]{3,2,0,1:T(4,128)(2,1)} %bitcast.6), calls=%async_computation | async-start | bytes 3145728 | tf_op jit(solution)/shard_map/all_to_all | solution.py:103
  41.1 2.6 %convolution_convert_fusion.1 = bf16[1024,768]{1,0:T(8,128)(2,1)S(1)} fusion(bf16[1024,512]{1,0:T(8,128)(2,1)} %reshape.178, bf16[512,1536]{1,0:T(8,128)(2,1)} %param.13), kind=kOutput, calls=%fused_computation.27 | convolution fusion | flops 806092800 | bytes 3407872 | tf_op jit(solution)/shard_map/dot_general | solution.py:104
  43.8 3.1 %reshape.179 = bf16[256,4,3,4,64]{4,3,2,1,0:T(4,128)(2,1)} reshape(bf16[1024,768]{1,0:T(8,128)(2,1)S(1)} %convolution_convert_fusion.1) | data formatting | bytes 3145728 | tf_op jit(solution)/shard_map/reshape | solution.py:107
  46.9 4.5 %copy.86 = bf16[256,4,3,4,64]{0,4,3,1,2:T(8,128)(2,1)S(1)} copy(bf16[256,4,3,4,64]{4,3,2,1,0:T(4,128)(2,1)} %reshape.179) | data formatting | bytes 3145728 | tf_op jit(solution)/shard_map/reshape | solution.py:107
  53.0 3.3 %multiply_reduce_fusion = (f32[4,4,256]{2,1,0:T(4,128)S(1)}, f32[4,4,256,256]{2,3,1,0:T(8,128)}) fusion(f32[4,4,256]{2,1,0:T(4,128)S(1)} %get-tuple-element.10, f32[256,256]{0,1:T(8,128)S(1)} %compare_convert_fusion, f32[4,4,256,256]{2,3,1,0:T(8,128)S(1)} %get-tuple-element.11, bf16[4,256,4,64]{1,3,2,0:T(8,128)(2,1)S(1)} %bitcast.158, ...), kind=kOutput, calls=%fused_computation.5 | convolution fusion | flops 139456512 | bytes 9732096 | tf_op jit(solution)/shard_map/anhd,amhd->ahnm/dot_general | solution.py:45
  60.9 12.0 %all-to-all-done = bf16[1,256,4,768]{3,2,0,1:T(4,128)(2,1)} async-done(((bf16[1,256,4,768]{3,2,0,1:T(4,128)(2,1)}), bf16[1,256,4,768]{3,2,0,1:T(4,128)(2,1)}, u32[]{:S(2)}, u32[]{:S(2)}) %all-to-all-start) | async-done | bytes 1572896 | tf_op jit(solution)/shard_map/all_to_all | solution.py:103
  75.8 5.7 %reshape.181 = bf16[8,128,3,4,64]{4,3,2,0,1:T(4,128)(2,1)} reshape(bf16[1,8,32,4,768]{4,1,3,2,0:T(8,128)(2,1)} %copy.91) | data formatting | bytes 3145728 | tf_op jit(solution)/shard_map/reshape | solution.py:114
  81.5 4.3 %fusion.58 = (bf16[8,128,1,4,64]{4,3,2,0,1:T(4,128)(2,1)}, bf16[8,128,1,4,64]{4,3,2,0,1:T(4,128)(2,1)}, bf16[8,128,1,4,64]{4,3,2,0,1:T(4,128)(2,1)}) fusion(bf16[8,128,3,4,64]{4,3,2,0,1:T(4,128)(2,1)} %reshape.181), kind=kLoop, calls=%fused_computation.98 | loop fusion | bytes 3145728 | tf_op jit(solution)/shard_map/slice | solution.py:116
  87.7 2.6 %copy.127 = bf16[8,128,1,4,64]{1,4,3,0,2:T(8,128)(2,1)} copy(bf16[8,128,1,4,64]{4,3,2,0,1:T(4,128)(2,1)} %get-tuple-element.4) | data formatting | bytes 1048576
  94.8 2.3 copy.97
  97.0 12.8 %all-to-all-start.1 = ((bf16[1,8,128,256]{3,1,0,2:T(8,128)(2,1)}), bf16[1,8,128,256]{3,1,0,2:T(8,128)(2,1)}, u32[]{:S(2)}, u32[]{:S(2)}) async-start(bf16[1,8,128,256]{3,1,0,2:T(8,128)(2,1)} %copy.97), calls=%async_computation.1 | async-start | bytes 1048576 | tf_op jit(solution)/shard_map/all_to_all | solution.py:119
  109.9 2.9 %multiply_reduce_fusion.1 = (f32[8,4,128]{2,1,0:T(4,128)S(1)}, f32[8,4,128,128]{2,3,1,0:T(8,128)S(1)}) fusion(f32[8,4,128]{2,1,0:T(4,128)S(1)} %get-tuple-element.8, f32[128,128]{0,1:T(8,128)S(1)} %fusion.20, f32[8,4,128,128]{2,3,1,0:T(8,128)} %copy-done.7, bf16[8,128,4,64]{1,3,2,0:T(8,128)(2,1)} %copy.107, bf16[8,128,1,4,64]{1,4,3,0,2:T(8,128)(2,1)} %copy.127), kind=kOutput, calls=%fused_computation.18 | convolution fusion | flops 69726208 | bytes 5341184 | tf_op jit(solution)/shard_map/anhd,amhd->ahnm/dot_general | solution.py:45
  117.0 3.0 %copy.113 = bf16[1,8,128,768]{3,1,0,2:T(8,128)(2,1)} copy(bf16[1,8,128,768]{2,3,1,0:T(8,128)(2,1)} %bitcast.150) | data formatting | bytes 3145728 | tf_op jit(solution)/shard_map/reshape | solution.py:168
  120.0 7.6 %all-to-all-done.1 = bf16[1,8,128,256]{3,1,0,2:T(8,128)(2,1)} async-done(((bf16[1,8,128,256]{3,1,0,2:T(8,128)(2,1)}), bf16[1,8,128,256]{3,1,0,2:T(8,128)(2,1)}, u32[]{:S(2)}, u32[]{:S(2)}) %all-to-all-start.1) | async-done | bytes 524320 | tf_op jit(solution)/shard_map/all_to_all | solution.py:119
  127.6 5.0 %all-to-all-start.3 = ((bf16[1,8,128,768]{3,1,0,2:T(8,128)(2,1)}), bf16[1,8,128,768]{3,1,0,2:T(8,128)(2,1)}, u32[]{:S(2)}, u32[]{:S(2)}) async-start(bf16[1,8,128,768]{3,1,0,2:T(8,128)(2,1)} %copy.113), calls=%async_computation.3 | async-start | bytes 3145728 | tf_op jit(solution)/shard_map/all_to_all | solution.py:171
  132.6 3.2 %convolution_convert_fusion.6 = bf16[4,4,64,256]{3,2,1,0:T(8,128)(2,1)S(1)} fusion(bf16[4,256,3,4,64]{1,4,3,0,2:T(8,128)(2,1)S(1)} %bitcast.146, f32[4,4,256,256]{2,3,1,0:T(8,128)} %copy-done.2, f32[4,4,256]{2,1,0:T(4,128)S(1)} %get-tuple-element.10, f32[256,256]{0,1:T(8,128)S(1)} %compare_convert_fusion), kind=kOutput, calls=%fused_computation.41 | convolution fusion | flops 138674176 | bytes 5521408 | tf_op jit(solution)/shard_map/ahnm,amhd->anhd/dot_general | solution.py:35
  136.8 4.5 %multiply_convert_fusion = bf16[4,4,256,256]{2,3,1,0:T(8,128)(2,1)S(1)} fusion(f32[4,4,256,256]{2,3,1,0:T(8,128)} %get-tuple-element.15, f32[4,4,256]{2,1,0:T(4,128)S(1)} %get-tuple-element.14, f32[4,4,256]{2,1,0:T(4,128)S(1)} %get-tuple-element.10, f32[256,256]{0,1:T(8,128)S(1)} %compare_convert_fusion, f32[4,4,256,256]{2,3,1,0:T(8,128)} %copy-done.2), kind=kLoop, calls=%fused_computation.4 | loop fusion | flops 6291456 | bytes 10780672 | tf_op jit(solution)/shard_map/convert_element_type | solution.py:49
  145.0 4.3 %copy.103 = bf16[256,4,3,4,64]{4,3,2,1,0:T(4,128)(2,1)} copy(bf16[256,4,3,4,64]{0,4,3,1,2:T(8,128)(2,1)S(1)} %maximum_bitcast_fusion) | data formatting | bytes 3145728 | tf_op jit(solution)/shard_map/transpose | solution.py:149
  149.3 4.9 %reshape.186 = bf16[1024,768]{1,0:T(8,128)(2,1)S(1)} reshape(bf16[256,4,3,4,64]{4,3,2,1,0:T(4,128)(2,1)} %copy.103) | data formatting | bytes 3145728 | tf_op jit(solution)/shard_map/reshape | solution.py:150
  158.2 5.1 %all-to-all-done.3 = bf16[1,8,128,768]{3,1,0,2:T(8,128)(2,1)} async-done(((bf16[1,8,128,768]{3,1,0,2:T(8,128)(2,1)}), bf16[1,8,128,768]{3,1,0,2:T(8,128)(2,1)}, u32[]{:S(2)}, u32[]{:S(2)}) %all-to-all-start.3) | async-done | bytes 1572896 | tf_op jit(solution)/shard_map/all_to_all | solution.py:171
  166.9 2.8 %fusion.60 = f32[768,512]{1,0:T(8,128)S(1)} fusion(bf16[1024,768]{1,0:T(8,128)(2,1)} %reshape.189, bf16[1024,512]{1,0:T(8,128)(2,1)} %reshape.178), kind=kOutput, calls=%fused_computation.100 | convolution fusion | flops 805306368 | bytes 4194304 | tf_op jit(solution)/shard_map/tc,td->cd/dot_general | solution.py:177
  172.8 2.5 %collective-permute-done = bf16[16,64,512]{2,1,0:T(8,128)(2,1)S(1)} collective-permute-done((bf16[16,64,512]{2,1,0:T(8,128)(2,1)}, bf16[16,64,512]{2,1,0:T(8,128)(2,1)S(1)}, u32[]{:S(2)}, u32[]{:S(2)}) %collective-permute-start) | collective-permute-done | bytes 1048608 | tf_op jit(solution)/shard_map/ppermute | solution.py:206
  177.1 36.8 %all_to_all.68 = bf16[16,64,512]{2,1,0:T(8,128)(2,1)S(1)} all-to-all(bf16[16,64,512]{2,1,0:T(8,128)(2,1)S(1)} %fusion.7), channel_id=1, replica_groups=mesh['dp'=8,'zh'=4,'x'=4,'core'=2] {'zh','x'}, dimensions={0} | all-to-all | bytes 2097152 | tf_op jit(solution)/shard_map/all_to_all | solution.py:208
  214.0 6.9 %collective-permute-start.1 = (f32[64,512]{1,0:T(8,128)S(1)}, f32[64,512]{1,0:T(8,128)S(1)}, u32[]{:S(2)}, u32[]{:S(2)}) collective-permute-start(f32[64,512]{1,0:T(8,128)S(1)} %convert_reduce_fusion), channel_id=1, source_target_pairs={{0,32},{32,0},{64,96},{96,64},{128,160},{160,128},{192,224},{224,1... | collective-permute-start | bytes 393224 | tf_op jit(solution)/shard_map/ppermute | solution.py:213
  221.0 3.4 %collective-permute-done.1 = f32[64,512]{1,0:T(8,128)S(1)} collective-permute-done((f32[64,512]{1,0:T(8,128)S(1)}, f32[64,512]{1,0:T(8,128)S(1)}, u32[]{:S(2)}, u32[]{:S(2)}) %collective-permute-start.1) | collective-permute-done | bytes 131104 | tf_op jit(solution)/shard_map/ppermute | solution.py:213
  229.7 2.2 concatenate.21
  236.0 3.0 %collective-permute-start.3 = (f32[64,512]{1,0:T(8,128)S(1)}, f32[64,512]{1,0:T(8,128)S(1)}, u32[]{:S(2)}, u32[]{:S(2)}) collective-permute-start(f32[64,512]{1,0:T(8,128)S(1)} %add.47), channel_id=1, source_target_pairs={{0,128},{32,160},{64,192},{96,224},{128,0},{160,32},{192,64},{224,... | collective-permute-start | bytes 393224 | tf_op jit(solution)/shard_map/ppermute | solution.py:213
  239.0 2.7 %add_convert_fusion = bf16[1024,512]{1,0:T(8,128)(2,1)} fusion(f32[1024,512]{1,0:T(8,128)S(1)} %copy-done.6, bf16[512,512]{1,0:T(8,128)(2,1)S(1)} %copy-done, bf16[1024,256]{1,0:T(8,128)(2,1)} %concatenate.22, bf16[1024,256]{1,0:T(8,128)(2,1)S(1)} %concatenate.21), kind=kOutput, calls=%fused_computation.19 | convolution fusion | flops 540016640 | bytes 4718592 | tf_op jit(solution)/shard_map/dot_general | solution.py:127
  (114 shorter events, 61.2 us)
Async XLA Ops:
  0.6 1.4 copy-start
  3.8 14.4 %copy-start.23 = (s32[1,256,4]{1,2,0:T(4,128)S(1)}, s32[1,256,4]{1,2,0:T(4,128)}, u32[]{:S(2)}) copy-start(s32[1,256,4]{1,2,0:T(4,128)} %param.10) | copy-start | bytes 12292
  3.8 14.6 %copy-start.4 = (bf16[1,256,4,512]{3,2,1,0:T(4,128)(2,1)S(1)}, bf16[1,256,4,512]{3,2,1,0:T(4,128)(2,1)}, u32[]{:S(2)}) copy-start(bf16[1,256,4,512]{3,2,1,0:T(4,128)(2,1)} %param.9) | copy-start | bytes 3145732
  3.8 14.6 %copy-start.21 = (f32[512]{0:T(512)S(1)}, f32[512]{0:T(512)}, u32[]{:S(2)}) copy-start(f32[512]{0:T(512)} %param.11) | copy-start | bytes 6148
  5.2 15.9 %copy-start.9 = (bf16[1,256,4,512]{3,2,1,0:T(4,128)(2,1)}, bf16[1,256,4,512]{3,2,1,0:T(4,128)(2,1)S(1)}, u32[]{:S(2)}) copy-start(bf16[1,256,4,512]{3,2,1,0:T(4,128)(2,1)S(1)} %reshape.185) | copy-start | bytes 3145732
  6.4 14.7 %copy-start.24 = (f32[512]{0:T(512)S(1)}, f32[512]{0:T(512)}, u32[]{:S(2)}) copy-start(f32[512]{0:T(512)} %param.12) | copy-start | bytes 6148
  6.4 28.6 %all-to-all-start.2 = ((bf16[1,256,4,256]{3,2,0,1:T(4,128)(2,1)}), bf16[1,256,4,256]{3,2,0,1:T(4,128)(2,1)S(1)}, u32[]{:S(2)}, u32[]{:S(2)}) async-start(bf16[1,256,4,256]{3,2,0,1:T(4,128)(2,1)} %slice.63), calls=%async_computation.2 | async-start | bytes 1048576 | tf_op jit(solution)/shard_map/all_to_all | solution.py:151
  28.8 11.8 %copy-start.10 = (bf16[1,256,4,512]{3,2,1,0:T(4,128)(2,1)S(1)}, bf16[1,256,4,512]{3,2,1,0:T(4,128)(2,1)}, u32[]{:S(2)}) copy-start(bf16[1,256,4,512]{3,2,1,0:T(4,128)(2,1)} %copy-done.9) | copy-start | bytes 3145732
  35.0 37.9 %all-to-all-start = ((bf16[1,256,4,768]{3,2,0,1:T(4,128)(2,1)}), bf16[1,256,4,768]{3,2,0,1:T(4,128)(2,1)}, u32[]{:S(2)}, u32[]{:S(2)}) async-start(bf16[1,256,4,768]{3,2,0,1:T(4,128)(2,1)} %bitcast.6), calls=%async_computation | async-start | bytes 3145728 | tf_op jit(solution)/shard_map/all_to_all | solution.py:103
  41.1 11.9 %copy-start.18 = (bf16[1,256,4,256]{1,3,2,0:T(8,128)(2,1)}, bf16[1,256,4,256]{1,3,2,0:T(8,128)(2,1)S(1)}, u32[]{:S(2)}) copy-start(bf16[1,256,4,256]{1,3,2,0:T(8,128)(2,1)S(1)} %copy.99) | copy-start | bytes 1572868
  46.9 4.5 %copy-start.25 = (s32[8,8]{1,0:T(8,128)S(1)}, s32[8,8]{1,0:T(8,128)}, u32[]{:S(2)}) copy-start(s32[8,8]{1,0:T(8,128)} %param.16) | copy-start | bytes 772
  46.9 4.9 %copy-start.22 = (s32[256]{0:T(256)S(1)}, s32[256]{0:T(256)}, u32[]{:S(2)}) copy-start(s32[256]{0:T(256)} %param.15) | copy-start | bytes 3076
  53.0 3.3 %copy-start.2 = (f32[4,4,256,256]{2,3,1,0:T(8,128)}, f32[4,4,256,256]{2,3,1,0:T(8,128)S(1)}, u32[]{:S(2)}) copy-start(f32[4,4,256,256]{2,3,1,0:T(8,128)S(1)} %get-tuple-element.11) | copy-start | bytes 12582916
  93.0 1.8 copy-start.7
  97.0 30.5 %all-to-all-start.1 = ((bf16[1,8,128,256]{3,1,0,2:T(8,128)(2,1)}), bf16[1,8,128,256]{3,1,0,2:T(8,128)(2,1)}, u32[]{:S(2)}, u32[]{:S(2)}) async-start(bf16[1,8,128,256]{3,1,0,2:T(8,128)(2,1)} %copy.97), calls=%async_computation.1 | async-start | bytes 1048576 | tf_op jit(solution)/shard_map/all_to_all | solution.py:119
  109.8 2.9 %copy-start.8 = (f32[8,4,128,128]{2,3,1,0:T(8,128)S(1)}, f32[8,4,128,128]{2,3,1,0:T(8,128)}, u32[]{:S(2)}) copy-start(f32[8,4,128,128]{2,3,1,0:T(8,128)} %copy-done.7) | copy-start | bytes 6291460
  127.6 35.8 %all-to-all-start.3 = ((bf16[1,8,128,768]{3,1,0,2:T(8,128)(2,1)}), bf16[1,8,128,768]{3,1,0,2:T(8,128)(2,1)}, u32[]{:S(2)}, u32[]{:S(2)}) async-start(bf16[1,8,128,768]{3,1,0,2:T(8,128)(2,1)} %copy.113), calls=%async_computation.3 | async-start | bytes 3145728 | tf_op jit(solution)/shard_map/all_to_all | solution.py:171
  135.8 5.5 %copy-start.11 = (bf16[4,4,64,256]{3,2,1,0:T(8,128)(2,1)}, bf16[4,4,64,256]{3,2,1,0:T(8,128)(2,1)S(1)}, u32[]{:S(2)}) copy-start(bf16[4,4,64,256]{3,2,1,0:T(8,128)(2,1)S(1)} %convolution_convert_fusion.6) | copy-start | bytes 1572868
  141.3 2.2 copy-start.3
  142.1 1.7 copy-start.19
  149.3 4.9 %copy-start.15 = (bf16[1024,512]{1,0:T(8,128)(2,1)S(1)}, bf16[1024,512]{1,0:T(8,128)(2,1)}, u32[]{:S(2)}) copy-start(bf16[1024,512]{1,0:T(8,128)(2,1)} %reshape.178) | copy-start | bytes 3145732
  154.2 3.3 %copy-start.14 = (bf16[1,256,4,512]{3,2,1,0:T(4,128)(2,1)S(1)}, bf16[1,256,4,512]{3,2,1,0:T(4,128)(2,1)}, u32[]{:S(2)}) copy-start(bf16[1,256,4,512]{3,2,1,0:T(4,128)(2,1)} %param.17) | copy-start | bytes 3145732
  154.2 3.3 %copy-start.20 = (bf16[1,256,4,256]{3,1,2,0:T(8,128)(2,1)S(1)}, bf16[1,256,4,256]{3,1,2,0:T(8,128)(2,1)}, u32[]{:S(2)}) copy-start(bf16[1,256,4,256]{3,1,2,0:T(8,128)(2,1)} %copy.116) | copy-start | bytes 1572868
  166.9 2.8 %copy-start.13 = (f32[768,512]{1,0:T(8,128)S(1)}, f32[768,512]{1,0:T(8,128)}, u32[]{:S(2)}) copy-start(f32[768,512]{1,0:T(8,128)} %fusion.59) | copy-start | bytes 4718596
  170.1 2.0 copy-start.1
  172.0 3.3 %collective-permute-start = (bf16[16,64,512]{2,1,0:T(8,128)(2,1)}, bf16[16,64,512]{2,1,0:T(8,128)(2,1)S(1)}, u32[]{:S(2)}, u32[]{:S(2)}) collective-permute-start(bf16[16,64,512]{2,1,0:T(8,128)(2,1)} %fusion.23), channel_id=1, source_target_pairs={{0,1},{1,0},{2,3},{3,2},{4,5},{5,4},{6,7},{7,6},{8,9},{9,8},{10,11... | collective-permute-start | bytes 3145736 | tf_op jit(solution)/shard_map/ppermute | solution.py:206
  177.0 49.3 %copy-start.5 = (f32[1,256,4,512]{3,2,1,0:T(4,128)S(1)}, f32[1,256,4,512]{3,2,1,0:T(4,128)}, u32[]{:S(2)}) copy-start(f32[1,256,4,512]{3,2,1,0:T(4,128)} %get-tuple-element.7) | copy-start | bytes 6291460
  214.0 10.3 %collective-permute-start.1 = (f32[64,512]{1,0:T(8,128)S(1)}, f32[64,512]{1,0:T(8,128)S(1)}, u32[]{:S(2)}, u32[]{:S(2)}) collective-permute-start(f32[64,512]{1,0:T(8,128)S(1)} %convert_reduce_fusion), channel_id=1, source_target_pairs={{0,32},{32,0},{64,96},{96,64},{128,160},{160,128},{192,224},{224,1... | collective-permute-start | bytes 393224 | tf_op jit(solution)/shard_map/ppermute | solution.py:213
  224.4 11.6 %collective-permute-start.2 = (f32[64,512]{1,0:T(8,128)S(1)}, f32[64,512]{1,0:T(8,128)S(1)}, u32[]{:S(2)}, u32[]{:S(2)}) collective-permute-start(f32[64,512]{1,0:T(8,128)S(1)} %add.46), channel_id=1, source_target_pairs={{0,64},{32,96},{64,0},{96,32},{128,192},{160,224},{192,128},{224,1... | collective-permute-start | bytes 393224 | tf_op jit(solution)/shard_map/ppermute | solution.py:213
  226.3 1.7 copy-start.12
  229.7 9.3 %copy-start.6 = (f32[1024,512]{1,0:T(8,128)S(1)}, f32[1024,512]{1,0:T(8,128)}, u32[]{:S(2)}) copy-start(f32[1024,512]{1,0:T(8,128)} %reshape.177) | copy-start | bytes 6291460
  236.0 7.9 %collective-permute-start.3 = (f32[64,512]{1,0:T(8,128)S(1)}, f32[64,512]{1,0:T(8,128)S(1)}, u32[]{:S(2)}, u32[]{:S(2)}) collective-permute-start(f32[64,512]{1,0:T(8,128)S(1)} %add.47), channel_id=1, source_target_pairs={{0,128},{32,160},{64,192},{96,224},{128,0},{160,32},{192,64},{224,... | collective-permute-start | bytes 393224 | tf_op jit(solution)/shard_map/ppermute | solution.py:213
  (2 other events, 2.3 us)
where the time goes:
time: 247 us; the launch traced here: 245 us
  local copies, waits for them, and re-layouts  74.3 us (30%)
  starting transfers between devices  47.7 us (19%)
  waiting for transfers between devices  36.9 us (15%)
  blocking collectives  36.8 us (15%)
  matrix products  32.4 us (13%)
  other arithmetic  15.8 us (6%)
    all_to_all x1, blocking collectives, reduce_share(): lax.all_to_all(summed, ('zh', 'x'), split_axis=0, concat_axis=0, tiled=True)  36.8 us
    all_to_all x1, starting transfers between devices, shards(): lax.all_to_all(time_out, SEQ, split_axis=2, concat_axis=1, tiled=True)  12.8 us
    all_to_all x1, waiting for transfers between devices, shards(): lax.all_to_all(time_part, SEQ, split_axis=1, concat_axis=2, tiled=True)  12 us
    ppermute x3, starting transfers between devices, reduce_share(): summed = summed + lax.ppermute(summed, 'dp', pairs)  11.8 us
    all_to_all x1, starting transfers between devices, shards(): lax.all_to_all(attended_grad[..., half_width:], SEQ, split_axis=1, concat...  11.7 us
    unnamed x55, local copies, waits for them, and re-layouts  8.8 us
    reshape x2, local copies, waits for them, and re-layouts, shards(): projected.reshape(electrodes, local_patches, 3, heads_half, HEAD_DIM)  7.64 us
    all_to_all x1, waiting for transfers between devices, shards(): lax.all_to_all(time_out, SEQ, split_axis=2, concat_axis=1, tiled=True)  7.58 us
  transfers between devices with their start and end apart: 8, of which 6 were waited for; matrix products, arithmetic and copies ran while one was open for 32% of the time, Pallas kernels for 0%

commit v1 on v0

--- a/solution.py
+++ b/solution.py
@@ -180,7 +180,7 @@
     qkv_grad = jnp.concatenate([space_qkv_grad, time_qkv_grad], axis=0)
     groups = lax.axis_size(SEQ)
     grad_scale = 1.0 / math.sqrt(
-        record_count * lax.axis_size("dp") * electrodes * local_patches * groups
+        record_count * lax.axis_size(DP) * electrodes * local_patches * groups
     )
     rows_qkv = qkv_grad.shape[0] // groups
     rows_out = model_width // groups
@@ -191,7 +191,7 @@
         ],
         axis=1,
     )
-    share = reduce_share(stacked, groups, lax.axis_size("dp"))
+    share = reduce_share(stacked, groups, lax.axis_size(DP))
     return (layer_out, share[:rows_qkv] * grad_scale, share[rows_qkv:] * grad_scale)
 
 
@@ -207,36 +207,36 @@
     summed = (keep + swapped.astype(jnp.float32)).astype(jnp.bfloat16)
     gathered = lax.all_to_all(summed, ("zh", "x"), split_axis=0, concat_axis=0, tiled=True)
     summed = jnp.sum(gathered.astype(jnp.float32), axis=0)
-    bit = 1
-    while bit < members:
-        pairs = [(i, i ^ bit) for i in range(members)]
-        summed = summed + lax.ppermute(summed, "dp", pairs)
-        bit *= 2
-    return summed
+    summed = summed + lax.ppermute(summed, "zl", [(0, 1), (1, 0)])
+    ys = lax.axis_size("y")
+    copies = jnp.broadcast_to(summed[None], (ys,) + summed.shape)
+    copies = lax.all_to_all(copies, "y", split_axis=0, concat_axis=0, tiled=True)
+    return jnp.sum(copies, axis=0)
 
 
 SEQ = ("zh", "x", "core")
+DP = ("y", "zl")
 
 
 def solution(mesh):
     dp_size, seq_size = mesh.devices.shape
     split = jax.sharding.Mesh(
-        mesh.devices.reshape(dp_size, seq_size // 8, 4, 2), ("dp",) + SEQ
+        mesh.devices.reshape(dp_size // 2, 2, seq_size // 8, 4, 2), DP + SEQ
     )
     return jax.shard_map(
         shards,
         mesh=split,
         in_specs=(
-            P("dp", None, SEQ, None),
-            P("dp", None, SEQ),
-            P(),
-            P(),
-            P(),
-            P(),
-            P(),
-            P(),
-            P("dp", None, SEQ, None),
+            P(DP, None, SEQ, None),
+            P(DP, None, SEQ),
+            P(),
+            P(),
+            P(),
+            P(),
+            P(),
+            P(),
+            P(DP, None, SEQ, None),
         ),
-        out_specs=(P("dp", None, SEQ, None), P(SEQ, None), P(SEQ, None)),
+        out_specs=(P(DP, None, SEQ, None), P(SEQ, None), P(SEQ, None)),
         check_vma=False,
     )

time: 247 us -> 249 us (level)
    ppermute x3 -> x1, starting transfers between devices: 11.8 us -> 6.93 us  [reduce_share(): summed = summed + lax.ppermute(summed, 'zl', [(0, 1), (1, 0)])]
    all_to_all x0 -> x1, starting transfers between devices: none -> 4.47 us  [reduce_share(): lax.all_to_all(copies, 'y', split_axis=0, concat_axis=0, tiled=True)]
  transfers between devices with their start and end apart: 8 -> 7, of which waited for: 6 -> 6; matrix products, arithmetic and copies ran while one was open for 32% -> 32% of each run, Pallas kernels for 0% -> 0%
where the time goes in v1:
time: 249 us; the launch traced here: 247 us
  local copies, waits for them, and re-layouts  75.2 us (30%)
  starting transfers between devices  47.3 us (19%)
  waiting for transfers between devices  36.8 us (15%)
  blocking collectives  36.8 us (15%)
  matrix products  32.4 us (13%)
  other arithmetic  16.9 us (7%)
    all_to_all x1, blocking collectives, reduce_share(): lax.all_to_all(summed, ('zh', 'x'), split_axis=0, concat_axis=0, tiled=True)  36.8 us
    all_to_all x1, starting transfers between devices, shards(): lax.all_to_all(time_out, SEQ, split_axis=2, concat_axis=1, tiled=True)  12.8 us
    all_to_all x1, waiting for transfers between devices, shards(): lax.all_to_all(time_part, SEQ, split_axis=1, concat_axis=2, tiled=True)  12 us
    all_to_all x1, starting transfers between devices, shards(): lax.all_to_all(attended_grad[..., half_width:], SEQ, split_axis=1, concat...  11.7 us
    unnamed x55, local copies, waits for them, and re-layouts  8.81 us
    reshape x2, local copies, waits for them, and re-layouts, shards(): projected.reshape(electrodes, local_patches, 3, heads_half, HEAD_DIM)  7.64 us
    all_to_all x1, waiting for transfers between devices, shards(): lax.all_to_all(time_out, SEQ, split_axis=2, concat_axis=1, tiled=True)  7.58 us
    ppermute x1, starting transfers between devices, reduce_share(): summed = summed + lax.ppermute(summed, 'zl', [(0, 1), (1, 0)])  6.93 us
  transfers between devices with their start and end apart: 7, of which 6 were waited for; matrix products, arithmetic and copies ran while one was open for 32% of the time, Pallas kernels for 0%

profile of v1, /device:TPU:2, one launch (start us, length us, event | category | flops | bytes accessed | tf_op | source)
XLA Modules:
  0.0 246.6 jit_solution(12947449021096624970)
XLA Ops:
  6.4 11.7 %all-to-all-start.2 = ((bf16[1,256,4,256]{3,2,0,1:T(4,128)(2,1)}), bf16[1,256,4,256]{3,2,0,1:T(4,128)(2,1)S(1)}, u32[]{:S(2)}, u32[]{:S(2)}) async-start(bf16[1,256,4,256]{3,2,0,1:T(4,128)(2,1)} %slice.63), calls=%async_computation.2 | async-start | bytes 1048576 | tf_op jit(solution)/shard_map/all_to_all | solution.py:151
  21.1 2.7 %multiply_convert_fusion.2 = (bf16[1,256,4,512]{3,2,1,0:T(4,128)(2,1)S(1)}, f32[1,256,4,512]{3,2,1,0:T(4,128)}) fusion(f32[512]{0:T(512)S(1)} %copy-done.24, f32[256,4]{1,0:T(8,128)S(1)} %add_rsqrt_fusion, f32[256,4]{1,0:T(8,128)S(1)} %broadcast_multiply_fusion, bf16[1,256,4,512]{3,2,1,0:T(4,128)(2,1)S(1)} %copy-done.4, f32[512]{0:T(512)S(1)} %copy-done.21, ...), kind=kLoop, calls=%fused_computation.21 | loop fusion | flops 3145728 | bytes 4207616 | tf_op jit(solution)/shard_map/convert_element_type | solution.py:23
  25.0 2.4 convolution_convert_fusion
  28.8 6.2 %all-to-all-done.2 = bf16[1,256,4,256]{3,2,0,1:T(4,128)(2,1)S(1)} async-done(((bf16[1,256,4,256]{3,2,0,1:T(4,128)(2,1)}), bf16[1,256,4,256]{3,2,0,1:T(4,128)(2,1)S(1)}, u32[]{:S(2)}, u32[]{:S(2)}) %all-to-all-start.2) | async-done | bytes 524320 | tf_op jit(solution)/shard_map/all_to_all | solution.py:151
  35.0 5.6 %all-to-all-start = ((bf16[1,256,4,768]{3,2,0,1:T(4,128)(2,1)}), bf16[1,256,4,768]{3,2,0,1:T(4,128)(2,1)}, u32[]{:S(2)}, u32[]{:S(2)}) async-start(bf16[1,256,4,768]{3,2,0,1:T(4,128)(2,1)} %bitcast.6), calls=%async_computation | async-start | bytes 3145728 | tf_op jit(solution)/shard_map/all_to_all | solution.py:103
  41.1 2.6 %convolution_convert_fusion.1 = bf16[1024,768]{1,0:T(8,128)(2,1)S(1)} fusion(bf16[1024,512]{1,0:T(8,128)(2,1)} %reshape.179, bf16[512,1536]{1,0:T(8,128)(2,1)} %param.13), kind=kOutput, calls=%fused_computation.27 | convolution fusion | flops 806092800 | bytes 3407872 | tf_op jit(solution)/shard_map/dot_general | solution.py:104
  43.8 3.1 %reshape.180 = bf16[256,4,3,4,64]{4,3,2,1,0:T(4,128)(2,1)} reshape(bf16[1024,768]{1,0:T(8,128)(2,1)S(1)} %convolution_convert_fusion.1) | data formatting | bytes 3145728 | tf_op jit(solution)/shard_map/reshape | solution.py:107
  46.9 4.5 %copy.119 = bf16[256,4,3,4,64]{0,4,3,1,2:T(8,128)(2,1)S(1)} copy(bf16[256,4,3,4,64]{4,3,2,1,0:T(4,128)(2,1)} %reshape.180) | data formatting | bytes 3145728 | tf_op jit(solution)/shard_map/reshape | solution.py:107
  53.0 3.2 %multiply_reduce_fusion = (f32[4,4,256]{2,1,0:T(4,128)S(1)}, f32[4,4,256,256]{2,3,1,0:T(8,128)}) fusion(f32[4,4,256]{2,1,0:T(4,128)S(1)} %get-tuple-element.10, f32[256,256]{0,1:T(8,128)S(1)} %compare_convert_fusion, f32[4,4,256,256]{2,3,1,0:T(8,128)S(1)} %get-tuple-element.11, bf16[4,256,4,64]{1,3,2,0:T(8,128)(2,1)S(1)} %bitcast.158, ...), kind=kOutput, calls=%fused_computation.5 | convolution fusion | flops 139456512 | bytes 9732096 | tf_op jit(solution)/shard_map/anhd,amhd->ahnm/dot_general | solution.py:45
  60.9 12.0 %all-to-all-done = bf16[1,256,4,768]{3,2,0,1:T(4,128)(2,1)} async-done(((bf16[1,256,4,768]{3,2,0,1:T(4,128)(2,1)}), bf16[1,256,4,768]{3,2,0,1:T(4,128)(2,1)}, u32[]{:S(2)}, u32[]{:S(2)}) %all-to-all-start) | async-done | bytes 1572896 | tf_op jit(solution)/shard_map/all_to_all | solution.py:103
  75.9 5.7 %reshape.182 = bf16[8,128,3,4,64]{4,3,2,0,1:T(4,128)(2,1)} reshape(bf16[1,8,32,4,768]{4,1,3,2,0:T(8,128)(2,1)} %copy.124) | data formatting | bytes 3145728 | tf_op jit(solution)/shard_map/reshape | solution.py:114
  81.6 4.3 %fusion.58 = (bf16[8,128,1,4,64]{4,3,2,0,1:T(4,128)(2,1)}, bf16[8,128,1,4,64]{4,3,2,0,1:T(4,128)(2,1)}, bf16[8,128,1,4,64]{4,3,2,0,1:T(4,128)(2,1)}) fusion(bf16[8,128,3,4,64]{4,3,2,0,1:T(4,128)(2,1)} %reshape.182), kind=kLoop, calls=%fused_computation.98 | loop fusion | bytes 3145728 | tf_op jit(solution)/shard_map/slice | solution.py:116
  87.8 2.6 %copy.160 = bf16[8,128,1,4,64]{1,4,3,0,2:T(8,128)(2,1)} copy(bf16[8,128,1,4,64]{4,3,2,0,1:T(4,128)(2,1)} %get-tuple-element.4) | data formatting | bytes 1048576
  94.8 2.2 copy.130
  97.0 12.8 %all-to-all-start.1 = ((bf16[1,8,128,256]{3,1,0,2:T(8,128)(2,1)}), bf16[1,8,128,256]{3,1,0,2:T(8,128)(2,1)}, u32[]{:S(2)}, u32[]{:S(2)}) async-start(bf16[1,8,128,256]{3,1,0,2:T(8,128)(2,1)} %copy.130), calls=%async_computation.1 | async-start | bytes 1048576 | tf_op jit(solution)/shard_map/all_to_all | solution.py:119
  109.9 2.9 %multiply_reduce_fusion.1 = (f32[8,4,128]{2,1,0:T(4,128)S(1)}, f32[8,4,128,128]{2,3,1,0:T(8,128)S(1)}) fusion(f32[8,4,128]{2,1,0:T(4,128)S(1)} %get-tuple-element.8, f32[128,128]{0,1:T(8,128)S(1)} %fusion.20, f32[8,4,128,128]{2,3,1,0:T(8,128)} %copy-done.7, bf16[8,128,4,64]{1,3,2,0:T(8,128)(2,1)} %copy.140, bf16[8,128,1,4,64]{1,4,3,0,2:T(8,128)(2,1)} %copy.160), kind=kOutput, calls=%fused_computation.18 | convolution fusion | flops 69726208 | bytes 5341184 | tf_op jit(solution)/shard_map/anhd,amhd->ahnm/dot_general | solution.py:45
  117.0 3.0 %copy.146 = bf16[1,8,128,768]{3,1,0,2:T(8,128)(2,1)} copy(bf16[1,8,128,768]{2,3,1,0:T(8,128)(2,1)} %bitcast.150) | data formatting | bytes 3145728 | tf_op jit(solution)/shard_map/reshape | solution.py:168
  120.0 7.6 %all-to-all-done.1 = bf16[1,8,128,256]{3,1,0,2:T(8,128)(2,1)} async-done(((bf16[1,8,128,256]{3,1,0,2:T(8,128)(2,1)}), bf16[1,8,128,256]{3,1,0,2:T(8,128)(2,1)}, u32[]{:S(2)}, u32[]{:S(2)}) %all-to-all-start.1) | async-done | bytes 524320 | tf_op jit(solution)/shard_map/all_to_all | solution.py:119
  127.6 5.0 %all-to-all-start.3 = ((bf16[1,8,128,768]{3,1,0,2:T(8,128)(2,1)}), bf16[1,8,128,768]{3,1,0,2:T(8,128)(2,1)}, u32[]{:S(2)}, u32[]{:S(2)}) async-start(bf16[1,8,128,768]{3,1,0,2:T(8,128)(2,1)} %copy.146), calls=%async_computation.3 | async-start | bytes 3145728 | tf_op jit(solution)/shard_map/all_to_all | solution.py:171
  132.6 3.2 %convolution_convert_fusion.6 = bf16[4,4,64,256]{3,2,1,0:T(8,128)(2,1)S(1)} fusion(bf16[4,256,3,4,64]{1,4,3,0,2:T(8,128)(2,1)S(1)} %bitcast.146, f32[4,4,256,256]{2,3,1,0:T(8,128)} %copy-done.2, f32[4,4,256]{2,1,0:T(4,128)S(1)} %get-tuple-element.10, f32[256,256]{0,1:T(8,128)S(1)} %compare_convert_fusion), kind=kOutput, calls=%fused_computation.41 | convolution fusion | flops 138674176 | bytes 5521408 | tf_op jit(solution)/shard_map/ahnm,amhd->anhd/dot_general | solution.py:35
  136.8 4.5 %multiply_convert_fusion = bf16[4,4,256,256]{2,3,1,0:T(8,128)(2,1)S(1)} fusion(f32[4,4,256,256]{2,3,1,0:T(8,128)} %get-tuple-element.15, f32[4,4,256]{2,1,0:T(4,128)S(1)} %get-tuple-element.14, f32[4,4,256]{2,1,0:T(4,128)S(1)} %get-tuple-element.10, f32[256,256]{0,1:T(8,128)S(1)} %compare_convert_fusion, f32[4,4,256,256]{2,3,1,0:T(8,128)} %copy-done.2), kind=kLoop, calls=%fused_computation.4 | loop fusion | flops 6291456 | bytes 10780672 | tf_op jit(solution)/shard_map/convert_element_type | solution.py:49
  145.0 4.3 %copy.136 = bf16[256,4,3,4,64]{4,3,2,1,0:T(4,128)(2,1)} copy(bf16[256,4,3,4,64]{0,4,3,1,2:T(8,128)(2,1)S(1)} %maximum_bitcast_fusion) | data formatting | bytes 3145728 | tf_op jit(solution)/shard_map/transpose | solution.py:149
  149.3 4.9 %reshape.187 = bf16[1024,768]{1,0:T(8,128)(2,1)S(1)} reshape(bf16[256,4,3,4,64]{4,3,2,1,0:T(4,128)(2,1)} %copy.136) | data formatting | bytes 3145728 | tf_op jit(solution)/shard_map/reshape | solution.py:150
  158.3 5.1 %all-to-all-done.3 = bf16[1,8,128,768]{3,1,0,2:T(8,128)(2,1)} async-done(((bf16[1,8,128,768]{3,1,0,2:T(8,128)(2,1)}), bf16[1,8,128,768]{3,1,0,2:T(8,128)(2,1)}, u32[]{:S(2)}, u32[]{:S(2)}) %all-to-all-start.3) | async-done | bytes 1572896 | tf_op jit(solution)/shard_map/all_to_all | solution.py:171
  166.8 2.8 %fusion.60 = f32[768,512]{1,0:T(8,128)S(1)} fusion(bf16[1024,768]{1,0:T(8,128)(2,1)} %reshape.190, bf16[1024,512]{1,0:T(8,128)(2,1)} %reshape.179), kind=kOutput, calls=%fused_computation.100 | convolution fusion | flops 805306368 | bytes 4194304 | tf_op jit(solution)/shard_map/tc,td->cd/dot_general | solution.py:177
  172.7 2.5 %collective-permute-done = bf16[16,64,512]{2,1,0:T(8,128)(2,1)S(1)} collective-permute-done((bf16[16,64,512]{2,1,0:T(8,128)(2,1)}, bf16[16,64,512]{2,1,0:T(8,128)(2,1)S(1)}, u32[]{:S(2)}, u32[]{:S(2)}) %collective-permute-start) | collective-permute-done | bytes 1048608 | tf_op jit(solution)/shard_map/ppermute | solution.py:206
  177.0 36.8 %all_to_all.73 = bf16[16,64,512]{2,1,0:T(8,128)(2,1)S(1)} all-to-all(bf16[16,64,512]{2,1,0:T(8,128)(2,1)S(1)} %fusion.7), channel_id=1, replica_groups=mesh['y'=4,'zl'=2,'zh'=4,'x'=4,'core'=2] {'zh','x'}, dimensions={0} | all-to-all | bytes 2097152 | tf_op jit(solution)/shard_map/all_to_all | solution.py:208
  213.9 6.9 %collective-permute-start.1 = (f32[64,512]{1,0:T(8,128)S(1)}, f32[64,512]{1,0:T(8,128)S(1)}, u32[]{:S(2)}, u32[]{:S(2)}) collective-permute-start(f32[64,512]{1,0:T(8,128)S(1)} %convert_reduce_fusion), channel_id=1, source_target_pairs={{0,32},{32,0},{1,33},{33,1},{2,34},{34,2},{3,35},{35,3},{4,36},{36... | collective-permute-start | bytes 393224 | tf_op jit(solution)/shard_map/ppermute | solution.py:210
  220.8 3.4 %collective-permute-done.1 = f32[64,512]{1,0:T(8,128)S(1)} collective-permute-done((f32[64,512]{1,0:T(8,128)S(1)}, f32[64,512]{1,0:T(8,128)S(1)}, u32[]{:S(2)}, u32[]{:S(2)}) %collective-permute-start.1) | collective-permute-done | bytes 131104 | tf_op jit(solution)/shard_map/ppermute | solution.py:210
  225.1 4.5 %all-to-all-start.5 = ((f32[4,64,512]{2,1,0:T(8,128)}), f32[4,64,512]{2,1,0:T(8,128)}, u32[]{:S(2)}, u32[]{:S(2)}) async-start(f32[4,64,512]{2,1,0:T(8,128)} %broadcast_in_dim.16), calls=%async_computation.5 | async-start | bytes 1048576 | tf_op jit(solution)/shard_map/all_to_all | solution.py:213
  233.0 2.2 concatenate.21
  239.3 2.7 %add_convert_fusion = bf16[1024,512]{1,0:T(8,128)(2,1)} fusion(f32[1024,512]{1,0:T(8,128)S(1)} %copy-done.6, bf16[512,512]{1,0:T(8,128)(2,1)S(1)} %copy-done, bf16[1024,256]{1,0:T(8,128)(2,1)} %concatenate.22, bf16[1024,256]{1,0:T(8,128)(2,1)S(1)} %concatenate.21), kind=kOutput, calls=%fused_computation.19 | convolution fusion | flops 540016640 | bytes 4718592 | tf_op jit(solution)/shard_map/dot_general | solution.py:127
  (112 shorter events, 61.3 us)
Async XLA Ops:
  0.6 1.4 copy-start
  3.8 14.4 %copy-start.23 = (s32[1,256,4]{1,2,0:T(4,128)S(1)}, s32[1,256,4]{1,2,0:T(4,128)}, u32[]{:S(2)}) copy-start(s32[1,256,4]{1,2,0:T(4,128)} %param.10) | copy-start | bytes 12292
  3.8 14.6 %copy-start.4 = (bf16[1,256,4,512]{3,2,1,0:T(4,128)(2,1)S(1)}, bf16[1,256,4,512]{3,2,1,0:T(4,128)(2,1)}, u32[]{:S(2)}) copy-start(bf16[1,256,4,512]{3,2,1,0:T(4,128)(2,1)} %param.9) | copy-start | bytes 3145732
  3.8 14.6 %copy-start.21 = (f32[512]{0:T(512)S(1)}, f32[512]{0:T(512)}, u32[]{:S(2)}) copy-start(f32[512]{0:T(512)} %param.11) | copy-start | bytes 6148
  5.2 15.9 %copy-start.9 = (bf16[1,256,4,512]{3,2,1,0:T(4,128)(2,1)}, bf16[1,256,4,512]{3,2,1,0:T(4,128)(2,1)S(1)}, u32[]{:S(2)}) copy-start(bf16[1,256,4,512]{3,2,1,0:T(4,128)(2,1)S(1)} %reshape.186) | copy-start | bytes 3145732
  6.4 14.7 %copy-start.24 = (f32[512]{0:T(512)S(1)}, f32[512]{0:T(512)}, u32[]{:S(2)}) copy-start(f32[512]{0:T(512)} %param.12) | copy-start | bytes 6148
  6.4 28.6 %all-to-all-start.2 = ((bf16[1,256,4,256]{3,2,0,1:T(4,128)(2,1)}), bf16[1,256,4,256]{3,2,0,1:T(4,128)(2,1)S(1)}, u32[]{:S(2)}, u32[]{:S(2)}) async-start(bf16[1,256,4,256]{3,2,0,1:T(4,128)(2,1)} %slice.63), calls=%async_computation.2 | async-start | bytes 1048576 | tf_op jit(solution)/shard_map/all_to_all | solution.py:151
  28.8 11.8 %copy-start.10 = (bf16[1,256,4,512]{3,2,1,0:T(4,128)(2,1)S(1)}, bf16[1,256,4,512]{3,2,1,0:T(4,128)(2,1)}, u32[]{:S(2)}) copy-start(bf16[1,256,4,512]{3,2,1,0:T(4,128)(2,1)} %copy-done.9) | copy-start | bytes 3145732
  35.0 37.9 %all-to-all-start = ((bf16[1,256,4,768]{3,2,0,1:T(4,128)(2,1)}), bf16[1,256,4,768]{3,2,0,1:T(4,128)(2,1)}, u32[]{:S(2)}, u32[]{:S(2)}) async-start(bf16[1,256,4,768]{3,2,0,1:T(4,128)(2,1)} %bitcast.6), calls=%async_computation | async-start | bytes 3145728 | tf_op jit(solution)/shard_map/all_to_all | solution.py:103
  41.1 11.9 %copy-start.18 = (bf16[1,256,4,256]{1,3,2,0:T(8,128)(2,1)}, bf16[1,256,4,256]{1,3,2,0:T(8,128)(2,1)S(1)}, u32[]{:S(2)}) copy-start(bf16[1,256,4,256]{1,3,2,0:T(8,128)(2,1)S(1)} %copy.132) | copy-start | bytes 1572868
  46.9 4.5 %copy-start.25 = (s32[8,8]{1,0:T(8,128)S(1)}, s32[8,8]{1,0:T(8,128)}, u32[]{:S(2)}) copy-start(s32[8,8]{1,0:T(8,128)} %param.16) | copy-start | bytes 772
  46.9 4.9 %copy-start.22 = (s32[256]{0:T(256)S(1)}, s32[256]{0:T(256)}, u32[]{:S(2)}) copy-start(s32[256]{0:T(256)} %param.15) | copy-start | bytes 3076
  53.0 3.3 %copy-start.2 = (f32[4,4,256,256]{2,3,1,0:T(8,128)}, f32[4,4,256,256]{2,3,1,0:T(8,128)S(1)}, u32[]{:S(2)}) copy-start(f32[4,4,256,256]{2,3,1,0:T(8,128)S(1)} %get-tuple-element.11) | copy-start | bytes 12582916
  93.0 1.8 copy-start.7
  97.0 30.5 %all-to-all-start.1 = ((bf16[1,8,128,256]{3,1,0,2:T(8,128)(2,1)}), bf16[1,8,128,256]{3,1,0,2:T(8,128)(2,1)}, u32[]{:S(2)}, u32[]{:S(2)}) async-start(bf16[1,8,128,256]{3,1,0,2:T(8,128)(2,1)} %copy.130), calls=%async_computation.1 | async-start | bytes 1048576 | tf_op jit(solution)/shard_map/all_to_all | solution.py:119
  109.9 2.9 %copy-start.8 = (f32[8,4,128,128]{2,3,1,0:T(8,128)S(1)}, f32[8,4,128,128]{2,3,1,0:T(8,128)}, u32[]{:S(2)}) copy-start(f32[8,4,128,128]{2,3,1,0:T(8,128)} %copy-done.7) | copy-start | bytes 6291460
  113.4 1.3 copy-start.16
  127.6 35.7 %all-to-all-start.3 = ((bf16[1,8,128,768]{3,1,0,2:T(8,128)(2,1)}), bf16[1,8,128,768]{3,1,0,2:T(8,128)(2,1)}, u32[]{:S(2)}, u32[]{:S(2)}) async-start(bf16[1,8,128,768]{3,1,0,2:T(8,128)(2,1)} %copy.146), calls=%async_computation.3 | async-start | bytes 3145728 | tf_op jit(solution)/shard_map/all_to_all | solution.py:171
  135.8 5.5 %copy-start.11 = (bf16[4,4,64,256]{3,2,1,0:T(8,128)(2,1)}, bf16[4,4,64,256]{3,2,1,0:T(8,128)(2,1)S(1)}, u32[]{:S(2)}) copy-start(bf16[4,4,64,256]{3,2,1,0:T(8,128)(2,1)S(1)} %convolution_convert_fusion.6) | copy-start | bytes 1572868
  141.3 2.2 copy-start.3
  142.1 1.7 copy-start.19
  149.3 4.9 %copy-start.15 = (bf16[1024,512]{1,0:T(8,128)(2,1)S(1)}, bf16[1024,512]{1,0:T(8,128)(2,1)}, u32[]{:S(2)}) copy-start(bf16[1024,512]{1,0:T(8,128)(2,1)} %reshape.179) | copy-start | bytes 3145732
  154.2 3.3 %copy-start.14 = (bf16[1,256,4,512]{3,2,1,0:T(4,128)(2,1)S(1)}, bf16[1,256,4,512]{3,2,1,0:T(4,128)(2,1)}, u32[]{:S(2)}) copy-start(bf16[1,256,4,512]{3,2,1,0:T(4,128)(2,1)} %param.17) | copy-start | bytes 3145732
  154.2 3.3 %copy-start.20 = (bf16[1,256,4,256]{3,1,2,0:T(8,128)(2,1)S(1)}, bf16[1,256,4,256]{3,1,2,0:T(8,128)(2,1)}, u32[]{:S(2)}) copy-start(bf16[1,256,4,256]{3,1,2,0:T(8,128)(2,1)} %copy.149) | copy-start | bytes 1572868
  166.8 2.8 %copy-start.13 = (f32[768,512]{1,0:T(8,128)S(1)}, f32[768,512]{1,0:T(8,128)}, u32[]{:S(2)}) copy-start(f32[768,512]{1,0:T(8,128)} %fusion.59) | copy-start | bytes 4718596
  170.0 2.0 copy-start.1
  172.0 3.2 %collective-permute-start = (bf16[16,64,512]{2,1,0:T(8,128)(2,1)}, bf16[16,64,512]{2,1,0:T(8,128)(2,1)S(1)}, u32[]{:S(2)}, u32[]{:S(2)}) collective-permute-start(bf16[16,64,512]{2,1,0:T(8,128)(2,1)} %fusion.23), channel_id=1, source_target_pairs={{0,1},{1,0},{2,3},{3,2},{4,5},{5,4},{6,7},{7,6},{8,9},{9,8},{10,11... | collective-permute-start | bytes 3145736 | tf_op jit(solution)/shard_map/ppermute | solution.py:206
  213.8 15.9 %copy-start.5 = (f32[1,256,4,512]{3,2,1,0:T(4,128)S(1)}, f32[1,256,4,512]{3,2,1,0:T(4,128)}, u32[]{:S(2)}) copy-start(f32[1,256,4,512]{3,2,1,0:T(4,128)} %get-tuple-element.7) | copy-start | bytes 6291460
  213.9 10.3 %collective-permute-start.1 = (f32[64,512]{1,0:T(8,128)S(1)}, f32[64,512]{1,0:T(8,128)S(1)}, u32[]{:S(2)}, u32[]{:S(2)}) collective-permute-start(f32[64,512]{1,0:T(8,128)S(1)} %convert_reduce_fusion), channel_id=1, source_target_pairs={{0,32},{32,0},{1,33},{33,1},{2,34},{34,2},{3,35},{35,3},{4,36},{36... | collective-permute-start | bytes 393224 | tf_op jit(solution)/shard_map/ppermute | solution.py:210
  225.1 19.1 %all-to-all-start.5 = ((f32[4,64,512]{2,1,0:T(8,128)}), f32[4,64,512]{2,1,0:T(8,128)}, u32[]{:S(2)}, u32[]{:S(2)}) async-start(f32[4,64,512]{2,1,0:T(8,128)} %broadcast_in_dim.16), calls=%async_computation.5 | async-start | bytes 1048576 | tf_op jit(solution)/shard_map/all_to_all | solution.py:213
  229.6 1.7 copy-start.12
  233.0 6.3 %copy-start.6 = (f32[1024,512]{1,0:T(8,128)S(1)}, f32[1024,512]{1,0:T(8,128)}, u32[]{:S(2)}) copy-start(f32[1024,512]{1,0:T(8,128)} %reshape.178) | copy-start | bytes 6291460
  (1 other events, 1.0 us)
